TPU v7x, 256 devices: a whole 4x4x8 slice. The times are simulated.
256 devices in a mesh: gx: 4 (over z_lo), gy: 8 (over z_hi, y), gz: 8 (over x, core).
Axes of the slice: x: 4, y: 4, z: 8 (z_hi: 2, z_lo: 4; z = z_hi * 4 + z_lo), core: 2. Of those that a mesh axis runs over, the one named last changes fastest.
Arguments:
- vectors: float32 [4, 5, 125, 4, 8, 1024], P(None, None, None, 'gx', 'gy', 'gz'), may hold values from -6 to 6
- stiffness: float32 [5, 5], replicated, may hold values from -2.5 to 2.5
- flux: float32 [3, 5, 5], replicated, may hold values from -1.25 to 1.25
- penalty: float32 [3, 5], replicated, may hold values from 0.2 to 2
- local_factor: float32 [5, 5], replicated, may hold values from -2.5 to 2.5
- element_field_factor: float32 [5, 5], replicated, may hold values from -2.5 to 2.5
- aggregate: int32 [4, 8, 1024], P('gx', 'gy', 'gz'), may hold values from 0 to 1023
- coarse_inverse: float32 [20480, 5120], P(('gx', 'gy', 'gz')), may hold values from -0.078125 to 0.078125
Outputs:
- result: float32 [4, 5, 125, 4, 8, 1024], P(None, None, None, 'gx', 'gy', 'gz')
Inputs may be any that keep to these rules, and one draw needn't show every extreme that they name: aggregate numbers are counted within the elements of one index of gx.
All inputs are finite; a program needn't handle non-finite values.
Results may differ from a plain program's by a relative error of at most 0.0001.
Values sent between devices are 32-bit elements; how exact they have to be, the bound alone decides.
No kernel may reach another device: no remote copies, remote signals or barrier semaphores. Data moves between devices by JAX's collectives and lax.ppermute only.
A program may use at most 256 MiB of HBM per device.

v0:
```python
import jax
import jax.numpy as jnp
import numpy as np
from jax import lax
from jax.sharding import PartitionSpec as P

HIGH = lax.Precision.HIGHEST


def with_halo(shard, sides, width):
    for axis, dim in sides:
        size, length = (lax.axis_size(axis), shard.shape[dim])
        up = [(i, (i + 1) % size) for i in range(size - 1)]
        down = [(j, i) for i, j in up]
        last = lax.slice_in_dim(shard, length - width, length, axis=dim)
        initial = lax.slice_in_dim(shard, 0, width, axis=dim)
        before = lax.ppermute(last, axis, up)
        after = lax.ppermute(initial, axis, down)
        shard = jnp.concatenate([before, shard, after], axis=dim)
    return shard


def kron_three(first, second, third):
    return jnp.kron(jnp.kron(first, second), third)


def operator_matrix(stiffness, flux):
    unit = jnp.eye(5, dtype=jnp.float32)
    sweeps = [
        kron_three(stiffness, unit, unit),
        kron_three(unit, stiffness, unit),
        kron_three(unit, unit, stiffness),
    ]
    total = jnp.zeros((625, 625), jnp.float32)
    for axis in range(3):
        total = total + jnp.kron(flux[axis], sweeps[axis])
    return total.reshape(5, 125, 5, 125)


def face_table():
    table = np.zeros((150, 125), np.float32)
    for axis in range(3):
        for side in range(2):
            level = 4 * side
            for first in range(5):
                for second in range(5):
                    if axis == 0:
                        node = 25 * level + 5 * first + second
                    elif axis == 1:
                        node = 25 * first + 5 * level + second
                    else:
                        node = 25 * first + 5 * second + level
                    table[50 * axis + 25 * side + 5 * first + second, node] = 1.0
    return table


def operate(flat, dims, big, penalty, selects):
    vecs, fields, elements = (flat.shape[0], flat.shape[1], flat.shape[3])
    output = flat + jnp.einsum("fqgp,kgpe->kfqe", big, flat, precision=HIGH)
    faces = jnp.einsum("sq,kfqe->kfse", selects, flat, precision=HIGH)
    shaped = (vecs, fields, 25) + dims
    pairs = []
    for axis in range(3):
        minus = faces[:, :, 50 * axis : 50 * axis + 25].reshape(shaped)
        plus = faces[:, :, 50 * axis + 25 : 50 * axis + 50].reshape(shaped)
        pairs.append((minus, plus))
    neighbours = []
    stacks = [jnp.stack([pairs[axis][0], pairs[axis][1]], 0) for axis in range(3)]
    outer = [
        with_halo(stacks[0], (("gx", 4),), 1),
        with_halo(stacks[1], (("gy", 5),), 1),
        with_halo(stacks[2], (("gz", 6),), 1),
    ]
    for axis in range(3):
        count = dims[axis]
        after = lax.slice_in_dim(outer[axis][0], 2, count + 2, axis=3 + axis)
        before = lax.slice_in_dim(outer[axis][1], 0, count, axis=3 + axis)
        neighbours.append((after, before))
    terms = []
    for axis in range(3):
        minus, plus = pairs[axis]
        tau = penalty[axis][None, :, None, None, None, None]
        terms.append((tau * (minus - neighbours[axis][1])).reshape(vecs, fields, 25, elements))
        terms.append((tau * (plus - neighbours[axis][0])).reshape(vecs, fields, 25, elements))
    stacked = jnp.concatenate(terms, axis=2)
    return output + jnp.einsum("sq,kfse->kfqe", selects, stacked, precision=HIGH)


def precondition(flat, local_kron, element_field_factor, onehot, coarse_inverse):
    vecs, fields, elements = (flat.shape[0], flat.shape[1], flat.shape[3])
    fine = jnp.einsum("qp,kfpe->kfqe", local_kron, flat, precision=HIGH)
    fine = jnp.einsum("fg,kgqe->kfqe", element_field_factor, fine, precision=HIGH)
    nagg = coarse_inverse.shape[1] // fields
    means = jnp.sum(flat, axis=2) * (1.0 / 125.0)
    block = means.reshape(vecs * fields, elements)
    partial_sum = jnp.dot(block, onehot, precision=HIGH)
    restricted = lax.psum(partial_sum, ("gy", "gz"))
    merged = restricted.reshape(vecs, fields * nagg)
    owned = jnp.einsum("kc,rc->kr", merged, coarse_inverse, precision=HIGH)
    coarse = lax.all_gather(owned, ("gy", "gz"), axis=1, tiled=True)
    values = jnp.dot(coarse.reshape(vecs * fields, nagg), onehot.T, precision=HIGH)
    back = values.reshape(vecs, fields, elements)
    return fine + back[:, :, None, :]


def on_device(
    vectors, stiffness, flux, penalty, local_factor, element_field_factor, aggregate, coarse_inverse
):
    big = operator_matrix(stiffness, flux)
    local_kron = kron_three(local_factor, local_factor, local_factor)
    selects = jnp.asarray(face_table())
    dims = tuple(vectors.shape[3:])
    elements = aggregate.size
    nagg = coarse_inverse.shape[1] // vectors.shape[1]
    onehot = (
        aggregate.reshape(elements)[:, None] == jnp.arange(nagg, dtype=jnp.int32)[None, :]
    ).astype(jnp.float32)
    flat = vectors.reshape(vectors.shape[:3] + (elements,))
    for turn in range(2):
        flat = precondition(flat, local_kron, element_field_factor, onehot, coarse_inverse)
        flat = operate(flat, dims, big, penalty, selects)
    return flat.reshape(vectors.shape)


def solution(mesh):
    placed = (
        P(None, None, None, "gx", "gy", "gz"),
        P(),
        P(),
        P(),
        P(),
        P(),
        P("gx", "gy", "gz"),
        P(("gx", "gy", "gz"), None),
    )
    return jax.shard_map(
        on_device,
        mesh=mesh,
        in_specs=placed,
        out_specs=P(None, None, None, "gx", "gy", "gz"),
        check_vma=False,
    )
```

profile of v0, /device:TPU:225, one launch (start us, length us, event | category | flops | bytes accessed | tf_op | source)
XLA Modules:
  0.0 1826.5 jit_solution(4462123117621494507)
XLA Ops:
  12.3 2.8 reshape.385
  15.1 2.5 convolution_bitcast_fusion.3
  19.8 2.6 broadcast_multiply_fusion.2
  23.6 3.4 mul.353
  27.0 3.4 mul.364
  30.4 3.4 mul.374
  34.4 687.8 %all-reduce.3.cloned.1.call-done = f32[4,5120]{1,0:T(4,128)} async-done(((f32[4,5120]{1,0:T(4,128)}), f32[4,5120]{1,0:T(4,128)}) %all-reduce.3.cloned.1.call-update) | async-done | bytes 81936 | tf_op jit(solution)/shard_map/psum | solution.py:97
  722.2 2.3 convolution_bitcast_fusion.5
  724.4 117.8 %all-gather = f32[64,80,4]{1,2,0:T(4,128)S(1)} all-gather(f32[1,80,4]{1,2,0:T(4,128)S(1)} %convolution_bitcast_fusion.5), channel_id=1, replica_groups=mesh['gx'=4,'gy'=8,'gz'=8] {'gy','gz'}, dimensions={0}, use_global_device_ids=true | all-gather | bytes 83200 | tf_op jit(solution)/shard_map/all_gather | solution.py:100
  842.9 2.5 bitcast_add_fusion.5
  852.5 9.4 collective-permute-start.3
  869.1 2.5 collective-permute-start.5
  876.3 4.6 fusion.9
  880.9 5.0 collective-permute-start.1
  893.5 2.8 collective-permute-done
  901.6 9.2 concatenate.27
  910.8 2.4 fusion.78
  913.2 4.3 fusion.76
  918.6 3.8 convolution_bitcast_fusion.2
  924.2 700.6 %all-reduce.5.cloned.1.call-done = f32[4,5120]{1,0:T(4,128)} async-done(((f32[4,5120]{1,0:T(4,128)}), f32[4,5120]{1,0:T(4,128)}) %all-reduce.5.cloned.1.call-update) | async-done | bytes 81936 | tf_op jit(solution)/shard_map/psum | solution.py:97
  1624.9 2.3 convolution_bitcast_fusion.4
  1627.1 118.0 %all-gather.1 = f32[64,80,4]{1,2,0:T(4,128)S(1)} all-gather(f32[1,80,4]{1,2,0:T(4,128)S(1)} %convolution_bitcast_fusion.4), channel_id=1, replica_groups=mesh['gx'=4,'gy'=8,'gz'=8] {'gy','gz'}, dimensions={0}, use_global_device_ids=true | all-gather | bytes 83200 | tf_op jit(solution)/shard_map/all_gather | solution.py:100
  1745.8 3.5 bitcast_add_fusion.2
  1755.6 9.4 collective-permute-start.9
  1773.6 2.4 collective-permute-start.11
  1776.0 6.2 fusion.12
  1782.2 5.0 collective-permute-start.7
  1793.9 5.4 collective-permute-done.6
  1804.1 3.3 concatenate.31
  1807.5 4.3 fusion.79
  1813.6 3.6 fusion
  1817.2 2.4 copy.89
  (175 shorter events, 73.5 us)
Async XLA Ops:
  6.5 715.7 %copy-start = (f32[80,5120]{1,0:T(8,128)S(1)}, f32[80,5120]{1,0:T(8,128)}, u32[]{:S(2)}) copy-start(f32[80,5120]{1,0:T(8,128)} %param.16) | copy-start | bytes 4915204
  6.5 715.7 %all-reduce.3.cloned.1.call-start = ((), (), s32[]{:S(2)}) async-start(), calls=%async_computation | async-start | bytes 163840 | tf_op jit(solution)/shard_map/psum | solution.py:97
  10.4 1614.5 %all-reduce.5.cloned.1.call-start = ((), (), s32[]{:S(2)}) async-start(), calls=%async_computation.1 | async-start | bytes 163840 | tf_op jit(solution)/shard_map/psum | solution.py:97
  23.6 876.7 %copy-start.25 = (f32[5]{0:T(128)}, f32[5]{0:T(128)S(1)}, u32[]{:S(2)}) copy-start(f32[5]{0:T(128)S(1)} %get-tuple-element.63) | copy-start | bytes 64
  23.6 876.7 %copy-start.28 = (f32[5]{0:T(128)}, f32[5]{0:T(128)S(1)}, u32[]{:S(2)}) copy-start(f32[5]{0:T(128)S(1)} %get-tuple-element.62) | copy-start | bytes 64
  33.8 808.6 %copy-start.37 = (s32[1,1,128]{2,1,0:T(1,128)S(1)}, s32[1,1,128]{2,1,0:T(1,128)}, u32[]{:S(2)}) copy-start(s32[1,1,128]{2,1,0:T(1,128)} %param.15) | copy-start | bytes 1540
  33.9 809.0 %copy-start.24 = (f32[5,5]{1,0:T(8,128)S(1)}, f32[5,5]{1,0:T(8,128)}, u32[]{:S(2)}) copy-start(f32[5,5]{1,0:T(8,128)} %param.14) | copy-start | bytes 304
  849.4 13.8 copy-start.6
  849.4 13.8 copy-start.9
  849.4 13.8 copy-start.10
  850.6 40.6 %collective-permute-start.2 = (f32[2,4,5,25,1,1,128]{6,1,5,4,3,2,0:T(4,128)}, f32[2,4,5,25,1,1,128]{6,1,5,4,3,2,0:T(4,128)}, u32[]{:S(2)}, u32[]{:S(2)}) collective-permute-start(f32[2,4,5,25,1,1,128]{6,1,5,4,3,2,0:T(4,128)} %copy.60), channel_id=1, source_target_pairs={{0,8},{8,16},{16,24},{24,32},{32,40},{40,48},{48,56},{1,9},{9,17},... | collective-permute-start | bytes 1536008 | tf_op jit(solution)/shard_map/ppermute | solution.py:17
  852.5 39.8 %collective-permute-start.3 = (f32[2,4,5,25,1,1,128]{6,1,5,4,3,2,0:T(4,128)}, f32[2,4,5,25,1,1,128]{6,1,5,4,3,2,0:T(4,128)}, u32[]{:S(2)}, u32[]{:S(2)}) collective-permute-start(f32[2,4,5,25,1,1,128]{6,1,5,4,3,2,0:T(4,128)} %copy.60), channel_id=1, source_target_pairs={{8,0},{16,8},{24,16},{32,24},{40,32},{48,40},{56,48},{9,1},{17,9},... | collective-permute-start | bytes 1536008 | tf_op jit(solution)/shard_map/ppermute | solution.py:18
  865.2 15.7 collective-permute-start.4
  869.1 7.1 copy-start.18
  869.1 7.1 copy-start.20
  869.1 7.1 copy-start.32
  869.1 7.1 copy-start.34
  869.1 7.1 copy-start.35
  869.1 17.9 collective-permute-start.5
  874.9 21.4 %collective-permute-start = (f32[2,4,5,25,1,1,128]{6,1,5,4,3,2,0:T(4,128)}, f32[2,4,5,25,1,1,128]{6,1,5,4,3,2,0:T(4,128)}, u32[]{:S(2)}, u32[]{:S(2)}) collective-permute-start(f32[2,4,5,25,1,1,128]{6,1,5,4,3,2,0:T(4,128)} %copy.54), channel_id=1, source_target_pairs={{0,64},{64,128},{128,192},{1,65},{65,129},{129,193},{2,66},{66,130... | collective-permute-start | bytes 1536008 | tf_op jit(solution)/shard_map/ppermute | solution.py:17
  880.9 17.0 collective-permute-start.1
  1752.5 15.0 copy-start.8
  1753.7 38.0 %collective-permute-start.8 = (f32[2,4,5,25,1,1,128]{6,1,5,4,3,2,0:T(4,128)}, f32[2,4,5,25,1,1,128]{6,1,5,4,3,2,0:T(4,128)}, u32[]{:S(2)}, u32[]{:S(2)}) collective-permute-start(f32[2,4,5,25,1,1,128]{6,1,5,4,3,2,0:T(4,128)} %copy.80), channel_id=1, source_target_pairs={{0,8},{8,16},{16,24},{24,32},{32,40},{40,48},{48,56},{1,9},{9,17},... | collective-permute-start | bytes 1536008 | tf_op jit(solution)/shard_map/ppermute | solution.py:17
  1755.6 37.2 %collective-permute-start.9 = (f32[2,4,5,25,1,1,128]{6,1,5,4,3,2,0:T(4,128)}, f32[2,4,5,25,1,1,128]{6,1,5,4,3,2,0:T(4,128)}, u32[]{:S(2)}, u32[]{:S(2)}) collective-permute-start(f32[2,4,5,25,1,1,128]{6,1,5,4,3,2,0:T(4,128)} %copy.80), channel_id=1, source_target_pairs={{8,0},{16,8},{24,16},{32,24},{40,32},{48,40},{56,48},{9,1},{17,9},... | collective-permute-start | bytes 1536008 | tf_op jit(solution)/shard_map/ppermute | solution.py:18
  1766.2 33.2 %collective-permute-start.6 = (f32[2,4,5,25,1,1,128]{6,1,5,4,3,2,0:T(4,128)}, f32[2,4,5,25,1,1,128]{6,1,5,4,3,2,0:T(4,128)}, u32[]{:S(2)}, u32[]{:S(2)}) collective-permute-start(f32[2,4,5,25,1,1,128]{6,1,5,4,3,2,0:T(4,128)} %copy.75), channel_id=1, source_target_pairs={{0,64},{64,128},{128,192},{1,65},{65,129},{129,193},{2,66},{66,130... | collective-permute-start | bytes 1536008 | tf_op jit(solution)/shard_map/ppermute | solution.py:17
  1767.5 8.5 copy-start.17
  1767.5 8.5 copy-start.19
  1767.5 8.5 copy-start.21
  1767.5 8.5 copy-start.33
  1770.2 11.9 collective-permute-start.10
  1773.6 14.8 collective-permute-start.11
  1782.2 18.7 %collective-permute-start.7 = (f32[2,4,5,25,1,1,128]{6,1,5,4,3,2,0:T(4,128)}, f32[2,4,5,25,1,1,128]{6,1,5,4,3,2,0:T(4,128)}, u32[]{:S(2)}, u32[]{:S(2)}) collective-permute-start(f32[2,4,5,25,1,1,128]{6,1,5,4,3,2,0:T(4,128)} %copy.75), channel_id=1, source_target_pairs={{64,0},{128,64},{192,128},{65,1},{129,65},{193,129},{66,2},{130,66... | collective-permute-start | bytes 1536008 | tf_op jit(solution)/shard_map/ppermute | solution.py:18
  (21 other events, 69.8 us)
Sparse Core Ops, SparseCore 0:
  10.5 711.6 all-reduce.2
  918.7 706.1 all-reduce.4
where the time goes:
time: 1840 us; the launch traced here: 1830 us
  waiting for transfers between devices  1400 us (76%)
  blocking collectives  236 us (13%)
  local copies, waits for them, and re-layouts  67.1 us (4%)
  starting transfers between devices  43.9 us (2%)
  matrix products  39.6 us (2%)
  other arithmetic  29 us (2%)
    psum x2, waiting for transfers between devices, precondition(): restricted = lax.psum(partial_sum, ('gy', 'gz'))  1390 us
    all_gather x2, blocking collectives, precondition(): coarse = lax.all_gather(owned, ('gy', 'gz'), axis=1, tiled=True)  236 us
  transfers between devices with their start and end apart: 14, of which 4 were waited for; matrix products, arithmetic and copies ran while one was open for 4% of the time, Pallas kernels for 0%

commit v1 on v0

--- a/solution.py
+++ b/solution.py
@@ -97,7 +97,9 @@
     restricted = lax.psum(partial_sum, ("gy", "gz"))
     merged = restricted.reshape(vecs, fields * nagg)
     owned = jnp.einsum("kc,rc->kr", merged, coarse_inverse, precision=HIGH)
-    coarse = lax.all_gather(owned, ("gy", "gz"), axis=1, tiled=True)
+    coarse = jnp.concatenate(
+        lax.all_to_all(jnp.stack([owned] * lax.axis_size(("gy", "gz"))), ("gy", "gz"), 0, 0), axis=1
+    )
     values = jnp.dot(coarse.reshape(vecs * fields, nagg), onehot.T, precision=HIGH)
     back = values.reshape(vecs, fields, elements)
     return fine + back[:, :, None, :]

time: 1840 us -> 1650 us (0.90)
  blocking collectives: 236 us -> 0 us
  starting transfers between devices: 43.9 us -> 71.1 us
    all_gather x2 -> x0, blocking collectives: 236 us -> none  [precondition(): coarse = lax.all_gather(owned, ('gy', 'gz'), axis=1, tiled=True)]
    all_to_all x0 -> x2, starting transfers between devices: none -> 24.9 us  [precondition(): lax.all_to_all(jnp.stack([owned] * lax.axis_size(('gy', 'gz'))), ('gy', '...]
  transfers between devices with their start and end apart: 14 -> 16, of which waited for: 4 -> 6; matrix products, arithmetic and copies ran while one was open for 4% -> 4% of each run, Pallas kernels for 0% -> 0%
where the time goes in v1:
time: 1650 us; the launch traced here: 1640 us
  waiting for transfers between devices  1410 us (85%)
  starting transfers between devices  71.1 us (4%)
  local copies, waits for them, and re-layouts  68.3 us (4%)
  matrix products  39.7 us (2%)
  other arithmetic  28.9 us (2%)
    psum x2, waiting for transfers between devices, precondition(): restricted = lax.psum(partial_sum, ('gy', 'gz'))  1400 us
  transfers between devices with their start and end apart: 16, of which 6 were waited for; matrix products, arithmetic and copies ran while one was open for 4% of the time, Pallas kernels for 0%

profile of v1, /device:TPU:225, one launch (start us, length us, event | category | flops | bytes accessed | tf_op | source)
XLA Modules:
  0.0 1635.0 jit_solution(15987375150177533768)
XLA Ops:
  12.3 2.8 reshape.391
  15.1 2.5 convolution_bitcast_fusion.3
  19.7 2.6 broadcast_multiply_fusion.2
  22.9 3.4 mul.353
  26.3 3.4 mul.364
  29.7 3.4 mul.374
  33.8 688.4 %all-reduce.3.cloned.1.call-done = f32[4,5120]{1,0:T(4,128)} async-done(((f32[4,5120]{1,0:T(4,128)}), f32[4,5120]{1,0:T(4,128)}) %all-reduce.3.cloned.1.call-update) | async-done | bytes 81936 | tf_op jit(solution)/shard_map/psum | solution.py:97
  722.2 2.3 fusion.78
  725.1 12.2 all-to-all-start
  738.2 6.5 all-to-all-done
  745.3 2.5 bitcast_add_fusion.5
  755.0 9.3 collective-permute-start.3
  767.6 3.3 collective-permute-start.4
  779.6 4.6 fusion.9
  784.2 5.0 collective-permute-start.1
  803.1 9.2 concatenate.27
  812.3 2.4 fusion.79
  814.7 4.2 fusion.76
  820.0 711.7 %all-reduce.5.cloned.1.call-done = f32[4,5120]{1,0:T(4,128)} async-done(((f32[4,5120]{1,0:T(4,128)}), f32[4,5120]{1,0:T(4,128)}) %all-reduce.5.cloned.1.call-update) | async-done | bytes 81936 | tf_op jit(solution)/shard_map/psum | solution.py:97
  1534.6 12.7 all-to-all-start.1
  1547.4 3.8 convolution_bitcast_fusion.2
  1555.2 3.5 bitcast_add_fusion.2
  1563.1 2.3 collective-permute-start.8
  1565.4 9.0 collective-permute-start.9
  1579.6 3.3 collective-permute-start.10
  1586.3 6.2 fusion.12
  1592.5 5.2 collective-permute-start.7
  1604.5 3.3 collective-permute-done.6
  1612.6 3.3 concatenate.31
  1615.9 4.3 fusion.81
  1622.0 3.6 fusion
  1625.6 2.4 copy.87
  (177 shorter events, 77.9 us)
Async XLA Ops:
  6.5 715.7 %copy-start = (f32[80,5120]{1,0:T(8,128)S(1)}, f32[80,5120]{1,0:T(8,128)}, u32[]{:S(2)}) copy-start(f32[80,5120]{1,0:T(8,128)} %param.16) | copy-start | bytes 4915204
  6.5 715.7 %all-reduce.3.cloned.1.call-start = ((), (), s32[]{:S(2)}) async-start(), calls=%async_computation.2 | async-start | bytes 163840 | tf_op jit(solution)/shard_map/psum | solution.py:97
  29.7 707.8 %copy-start.36 = (f32[3,5]{1,0:T(4,128)S(1)}, f32[3,5]{1,0:T(4,128)}, u32[]{:S(2)}) copy-start(f32[3,5]{1,0:T(4,128)} %param.12) | copy-start | bytes 184
  33.2 711.7 %copy-start.37 = (s32[1,1,128]{2,1,0:T(1,128)S(1)}, s32[1,1,128]{2,1,0:T(1,128)}, u32[]{:S(2)}) copy-start(s32[1,1,128]{2,1,0:T(1,128)} %param.15) | copy-start | bytes 1540
  33.2 712.1 %copy-start.24 = (f32[5,5]{1,0:T(8,128)S(1)}, f32[5,5]{1,0:T(8,128)}, u32[]{:S(2)}) copy-start(f32[5,5]{1,0:T(8,128)} %param.14) | copy-start | bytes 304
  725.1 19.6 %all-to-all-start = ((f32[64,4,80]{2,1,0:T(4,128)}), f32[64,4,80]{2,1,0:T(4,128)S(1)}, u32[]{:S(2)}, u32[]{:S(2)}) async-start(f32[64,4,80]{2,1,0:T(4,128)} %stack.16), calls=%async_computation | async-start | bytes 262144 | tf_op jit(solution)/shard_map/all_to_all | solution.py:101
  737.3 794.4 %all-reduce.5.cloned.1.call-start = ((), (), s32[]{:S(2)}) async-start(), calls=%async_computation.3 | async-start | bytes 163840 | tf_op jit(solution)/shard_map/psum | solution.py:97
  738.1 63.6 %copy-start.25 = (f32[5]{0:T(128)}, f32[5]{0:T(128)S(1)}, u32[]{:S(2)}) copy-start(f32[5]{0:T(128)S(1)} %get-tuple-element.63) | copy-start | bytes 64
  738.1 63.6 %copy-start.28 = (f32[5]{0:T(128)}, f32[5]{0:T(128)S(1)}, u32[]{:S(2)}) copy-start(f32[5]{0:T(128)S(1)} %get-tuple-element.62) | copy-start | bytes 64
  751.8 13.8 copy-start.6
  751.8 13.8 copy-start.9
  751.8 13.8 copy-start.10
  753.0 41.5 %collective-permute-start.2 = (f32[2,4,5,25,1,1,128]{6,1,5,4,3,2,0:T(4,128)}, f32[2,4,5,25,1,1,128]{6,1,5,4,3,2,0:T(4,128)}, u32[]{:S(2)}, u32[]{:S(2)}) collective-permute-start(f32[2,4,5,25,1,1,128]{6,1,5,4,3,2,0:T(4,128)} %copy.58), channel_id=1, source_target_pairs={{0,8},{8,16},{16,24},{24,32},{32,40},{40,48},{48,56},{1,9},{9,17},... | collective-permute-start | bytes 1536008 | tf_op jit(solution)/shard_map/ppermute | solution.py:17
  755.0 40.7 %collective-permute-start.3 = (f32[2,4,5,25,1,1,128]{6,1,5,4,3,2,0:T(4,128)}, f32[2,4,5,25,1,1,128]{6,1,5,4,3,2,0:T(4,128)}, u32[]{:S(2)}, u32[]{:S(2)}) collective-permute-start(f32[2,4,5,25,1,1,128]{6,1,5,4,3,2,0:T(4,128)} %copy.58), channel_id=1, source_target_pairs={{8,0},{16,8},{24,16},{32,24},{40,32},{48,40},{56,48},{9,1},{17,9},... | collective-permute-start | bytes 1536008 | tf_op jit(solution)/shard_map/ppermute | solution.py:18
  767.6 16.6 %collective-permute-start.4 = (f32[2,4,5,25,1,1,1]{3,1,6,5,4,2,0:T(4,128)}, f32[2,4,5,25,1,1,1]{3,1,6,5,4,2,0:T(4,128)S(1)}, u32[]{:S(2)}, u32[]{:S(2)}) collective-permute-start(f32[2,4,5,25,1,1,1]{3,1,6,5,4,2,0:T(4,128)} %copy.62), channel_id=1, source_target_pairs={{0,1},{1,2},{2,3},{3,4},{4,5},{5,6},{6,7},{8,9},{9,10},{10,11},{11... | collective-permute-start | bytes 12008 | tf_op jit(solution)/shard_map/ppermute | solution.py:17
  772.9 6.6 copy-start.32
  773.0 17.4 %collective-permute-start.5 = (f32[2,4,5,25,1,1,1]{3,1,6,5,4,2,0:T(4,128)}, f32[2,4,5,25,1,1,1]{3,1,6,5,4,2,0:T(4,128)}, u32[]{:S(2)}, u32[]{:S(2)}) collective-permute-start(f32[2,4,5,25,1,1,1]{3,1,6,5,4,2,0:T(4,128)} %copy.63), channel_id=1, source_target_pairs={{1,0},{2,1},{3,2},{4,3},{5,4},{6,5},{7,6},{9,8},{10,9},{11,10},{12... | collective-permute-start | bytes 12008 | tf_op jit(solution)/shard_map/ppermute | solution.py:18
  778.2 19.5 %collective-permute-start = (f32[2,4,5,25,1,1,128]{6,1,5,4,3,2,0:T(4,128)}, f32[2,4,5,25,1,1,128]{6,1,5,4,3,2,0:T(4,128)}, u32[]{:S(2)}, u32[]{:S(2)}) collective-permute-start(f32[2,4,5,25,1,1,128]{6,1,5,4,3,2,0:T(4,128)} %copy.52), channel_id=1, source_target_pairs={{0,64},{64,128},{128,192},{1,65},{65,129},{129,193},{2,66},{66,130... | collective-permute-start | bytes 1536008 | tf_op jit(solution)/shard_map/ppermute | solution.py:17
  784.2 15.1 collective-permute-start.1
  818.9 728.4 %copy-start.15 = (f32[125,125,1,1]{1,0,2,3:T(8,128)S(1)}, f32[125,125,1,1]{1,0,2,3:T(8,128)}, u32[]{:S(2)}) copy-start(f32[125,125,1,1]{1,0,2,3:T(8,128)} %copy-done.14) | copy-start | bytes 187504
  1534.6 20.0 %all-to-all-start.1 = ((f32[64,4,80]{2,1,0:T(4,128)}), f32[64,4,80]{2,1,0:T(4,128)S(1)}, u32[]{:S(2)}, u32[]{:S(2)}) async-start(f32[64,4,80]{2,1,0:T(4,128)} %stack.20), calls=%async_computation.1 | async-start | bytes 262144 | tf_op jit(solution)/shard_map/all_to_all | solution.py:101
  1561.9 15.0 copy-start.8
  1563.1 39.2 %collective-permute-start.8 = (f32[2,4,5,25,1,1,128]{6,1,5,4,3,2,0:T(4,128)}, f32[2,4,5,25,1,1,128]{6,1,5,4,3,2,0:T(4,128)}, u32[]{:S(2)}, u32[]{:S(2)}) collective-permute-start(f32[2,4,5,25,1,1,128]{6,1,5,4,3,2,0:T(4,128)} %copy.78), channel_id=1, source_target_pairs={{0,8},{8,16},{16,24},{24,32},{32,40},{40,48},{48,56},{1,9},{9,17},... | collective-permute-start | bytes 1536008 | tf_op jit(solution)/shard_map/ppermute | solution.py:17
  1565.4 38.0 %collective-permute-start.9 = (f32[2,4,5,25,1,1,128]{6,1,5,4,3,2,0:T(4,128)}, f32[2,4,5,25,1,1,128]{6,1,5,4,3,2,0:T(4,128)}, u32[]{:S(2)}, u32[]{:S(2)}) collective-permute-start(f32[2,4,5,25,1,1,128]{6,1,5,4,3,2,0:T(4,128)} %copy.78), channel_id=1, source_target_pairs={{8,0},{16,8},{24,16},{32,24},{40,32},{48,40},{56,48},{9,1},{17,9},... | collective-permute-start | bytes 1536008 | tf_op jit(solution)/shard_map/ppermute | solution.py:18
  1575.6 32.3 %collective-permute-start.6 = (f32[2,4,5,25,1,1,128]{6,1,5,4,3,2,0:T(4,128)}, f32[2,4,5,25,1,1,128]{6,1,5,4,3,2,0:T(4,128)}, u32[]{:S(2)}, u32[]{:S(2)}) collective-permute-start(f32[2,4,5,25,1,1,128]{6,1,5,4,3,2,0:T(4,128)} %copy.73), channel_id=1, source_target_pairs={{0,64},{64,128},{128,192},{1,65},{65,129},{129,193},{2,66},{66,130... | collective-permute-start | bytes 1536008 | tf_op jit(solution)/shard_map/ppermute | solution.py:17
  1576.9 9.4 copy-start.17
  1576.9 9.4 copy-start.19
  1576.9 9.4 copy-start.21
  1576.9 9.4 copy-start.33
  1579.6 12.9 collective-permute-start.10
  1584.4 14.6 collective-permute-start.11
  1592.5 16.9 %collective-permute-start.7 = (f32[2,4,5,25,1,1,128]{6,1,5,4,3,2,0:T(4,128)}, f32[2,4,5,25,1,1,128]{6,1,5,4,3,2,0:T(4,128)}, u32[]{:S(2)}, u32[]{:S(2)}) collective-permute-start(f32[2,4,5,25,1,1,128]{6,1,5,4,3,2,0:T(4,128)} %copy.73), channel_id=1, source_target_pairs={{64,0},{128,64},{192,128},{65,1},{129,65},{193,129},{66,2},{130,66... | collective-permute-start | bytes 1536008 | tf_op jit(solution)/shard_map/ppermute | solution.py:18
  (23 other events, 84.6 us)
Sparse Core Ops, SparseCore 0:
  10.5 711.6 all-reduce.2
  820.1 711.5 all-reduce.4
